TPU v7x, 512 devices: a whole 4x8x8 slice. The times are simulated.
512 devices in a mesh: seq: 64 (over z_hi, y, core), tp: 8 (over x, z_lo).
Axes of the slice: x: 4, y: 8, z: 8 (z_hi: 4, z_lo: 2; z = z_hi * 2 + z_lo), core: 2. Of those that a mesh axis runs over, the one named last changes fastest.
Arguments:
- query_proj: bfloat16 [16384, 3072], P('seq', 'tp'), may hold values from -8 to 8
- key_proj: bfloat16 [16384, 3072], P('seq', 'tp'), may hold values from -8 to 8
- value_proj: bfloat16 [16384, 3072], P('seq', 'tp'), may hold values from -6 to 6
- hidden: bfloat16 [16384, 3072], P('seq', 'tp'), may hold values from -2 to 2
- out_weight: bfloat16 [3072, 3072], P('tp'), may hold values from -0.109375 to 0.109375
- norm_gain: bfloat16 [3072], P('tp'), may hold values from 0.099609375 to 1.8984375
- segment_ids: int32 [16384], P('seq'), may hold values from 0 to 31, never falling along the last dimension, each value on 1 to 8192 neighbouring positions
- pad_mask: int32 [16384], P('seq'), may hold values 0 or 1
- page_table: int32 [128], P('seq'), may hold values from 0 to 1, as said below
Outputs:
- hidden_out: bfloat16 [16384, 3072], P('seq', 'tp')
- normed: bfloat16 [16384, 3072], P('seq', 'tp')
- kv_pages: bfloat16 [128, 2, 128, 3072], P('seq', None, None, 'tp')
Inputs may be any that keep to these rules, and one draw needn't show every extreme that they name: `segment_ids`: never falling along the tokens; each of the 32 prompts has 1 to 8192 tokens, one exactly 8192. `page_table`: the 2 pages of each aligned block of 2 pages name each slot once.
All inputs are finite; a program needn't handle non-finite values. No bound on the sum of `pad_mask` on one device may be relied on, other than what follows from the above.
Results may differ from a plain program's by a relative error of at most 0.014.
Values may be sent and summed in bfloat16 or wider, within the bound.
No kernel may reach another device: no remote copies, remote signals or barrier semaphores. Data moves between devices by JAX's collectives and lax.ppermute only.
A program may use at most 128 MiB of HBM per device.

v0:
```python
import math
import jax
import jax.numpy as jnp
from jax import lax
from jax.sharding import PartitionSpec as P

D = 3072
HEAD_DIM = 96
PAGE = 128
far_index = 1073741824
masked_score = -1e30
norm_epsilon = 1e-05


def passed_along(block, axis, distance):
    devices = range(lax.axis_size(axis))
    route = [(i - distance, i) for i in devices if i - distance in devices]
    return lax.ppermute(block, axis, route)


def rotate(values_in, position, head_count, head_dim):
    count_rows = values_in.shape[0]
    half_dim = head_dim // 2
    frequency = jnp.exp(
        jnp.arange(half_dim, dtype=jnp.float32) * (-2.0 * math.log(10000.0) / head_dim)
    )
    angles = position.astype(jnp.float32)[:, None] * frequency[None, :]
    cosine = jnp.cos(angles)[:, None, :]
    sine_part = jnp.sin(angles)[:, None, :]
    as_float = values_in.astype(jnp.float32).reshape(count_rows, head_count, head_dim)
    lower_half = as_float[..., :half_dim]
    upper_half = as_float[..., half_dim:]
    rotated = jnp.concatenate(
        [
            lower_half * cosine - upper_half * sine_part,
            upper_half * cosine + lower_half * sine_part,
        ],
        axis=-1,
    )
    return rotated.reshape(count_rows, head_count * head_dim).astype(jnp.bfloat16)


def attend(softmax_state, query_heads, block, visible):
    row_peak, row_total, weighted = softmax_state
    key_count = block.shape[1]
    head_count = query_heads.shape[1]
    key_heads = block[0].reshape(key_count, head_count, HEAD_DIM)
    val_heads = block[1].reshape(key_count, head_count, HEAD_DIM)
    factor = 1.0 / math.sqrt(HEAD_DIM)
    logits = (
        jnp.einsum("qhd,khd->hqk", query_heads, key_heads, preferred_element_type=jnp.float32)
        * factor
    )
    logits = jnp.where(visible[None], logits, masked_score)
    new_peak = jnp.maximum(row_peak, jnp.max(logits, axis=-1))
    rescale = jnp.exp(row_peak - new_peak)
    unnormed = jnp.where(visible[None], jnp.exp(logits - new_peak[..., None]), 0.0)
    row_total = row_total * rescale + jnp.sum(unnormed, axis=-1)
    weighted = weighted * rescale[..., None] + jnp.einsum(
        "hqk,khd->hqd", unnormed.astype(jnp.bfloat16), val_heads, preferred_element_type=jnp.float32
    )
    return (new_peak, row_total, weighted)


def per_device(
    query_proj,
    key_proj,
    value_proj,
    hidden,
    out_weight,
    norm_gain,
    segment_ids,
    pad_mask,
    page_table,
):
    tok_count = query_proj.shape[0]
    feat_count = query_proj.shape[1]
    head_count = feat_count // HEAD_DIM
    seg_count = lax.axis_size("seq") // 2
    reach_count = lax.axis_size("seq") // 2
    device_row = lax.axis_index("seq")
    tok_index = device_row * tok_count + jnp.arange(tok_count, dtype=jnp.int32)
    member = segment_ids[:, None] == jnp.arange(seg_count, dtype=jnp.int32)[None, :]
    local_first = jnp.min(jnp.where(member, tok_index[:, None], far_index), axis=0)
    first_tok = lax.pmin(local_first, "seq")
    position = tok_index - jnp.sum(jnp.where(member, first_tok[None, :], 0), axis=1)
    q_rot = rotate(query_proj, position, head_count, HEAD_DIM)
    k_rot = rotate(key_proj, position, head_count, HEAD_DIM)
    query_heads = q_rot.reshape(tok_count, head_count, HEAD_DIM)
    query_tag = segment_ids + 1
    key_tag = jnp.where(pad_mask == 1, segment_ids + 1, 0)
    own_block = jnp.stack([k_rot, value_proj])
    offsets = jnp.arange(tok_count, dtype=jnp.int32)
    own_visible = (key_tag[None, :] == query_tag[:, None]) & (
        offsets[None, :] <= offsets[:, None]
    ) | (offsets[None, :] == offsets[:, None])
    softmax_state = (
        jnp.full((head_count, tok_count), masked_score, jnp.float32),
        jnp.zeros((head_count, tok_count), jnp.float32),
        jnp.zeros((head_count, tok_count, HEAD_DIM), jnp.float32),
    )
    softmax_state = attend(softmax_state, query_heads, own_block, own_visible)

    def visit_block(current, moved, moved_tags):
        visible = moved_tags[None, :] == query_tag[:, None]
        return attend(current, query_heads, moved, visible)

    def cycle_turn(turn_index, loop_state):
        current, moved, moved_tags = loop_state
        moved, moved_tags = passed_along((moved, moved_tags), "seq", 1)
        return (visit_block(current, moved, moved_tags), moved, moved_tags)

    softmax_state = lax.fori_loop(0, reach_count, cycle_turn, (softmax_state, own_block, key_tag))[
        0
    ]
    row_peak, row_total, weighted = softmax_state
    attn = (
        jnp.transpose(weighted / row_total[..., None], (1, 0, 2))
        .reshape(tok_count, feat_count)
        .astype(jnp.bfloat16)
    )
    partial_value = jnp.dot(attn, out_weight, preferred_element_type=jnp.float32)
    feature_width = hidden.shape[1]
    summed = lax.psum(partial_value.astype(jnp.bfloat16), "tp").astype(jnp.float32)
    own_sum = lax.dynamic_slice_in_dim(
        summed, lax.axis_index("tp") * feature_width, feature_width, 1
    )
    hidden_out = (hidden.astype(jnp.float32) + own_sum).astype(jnp.bfloat16)
    stream_wide = hidden_out.astype(jnp.float32)
    square_total = lax.psum(jnp.sum(stream_wide * stream_wide, axis=1), "tp")
    normed = (
        stream_wide
        * lax.rsqrt(square_total / D + norm_epsilon)[:, None]
        * norm_gain.astype(jnp.float32)[None, :]
    ).astype(jnp.bfloat16)
    pad_scale = pad_mask.astype(jnp.bfloat16)[:, None]
    page_count = tok_count // PAGE
    stacked = jnp.stack([k_rot * pad_scale, value_proj * pad_scale])
    stacked = stacked.reshape(2, page_count, PAGE, feat_count).transpose(1, 0, 2, 3)
    kv_pages = jnp.zeros_like(stacked).at[page_table].set(stacked)
    return (hidden_out, normed, kv_pages)


def solution(mesh):
    placed = (
        P("seq", "tp"),
        P("seq", "tp"),
        P("seq", "tp"),
        P("seq", "tp"),
        P("tp", None),
        P("tp"),
        P("seq"),
        P("seq"),
        P("seq"),
    )
    return jax.shard_map(
        per_device,
        mesh=mesh,
        in_specs=placed,
        out_specs=(P("seq", "tp"), P("seq", "tp"), P("seq", None, None, "tp")),
        check_vma=False,
    )
```

profile of v0, /device:TPU:8, one launch (start us, length us, event | category | flops | bytes accessed | tf_op | source)
XLA Modules:
  0.0 713.5 jit_solution(16163749201808365648)
XLA Ops:
  8.2 28.3 %pmin.7 = s32[32]{0:T(128)S(1)} all-reduce(s32[32]{0:T(128)S(1)} %select_reduce_fusion.1), channel_id=1, replica_groups=mesh['seq'=64,'tp'=8] {'seq'}, use_global_device_ids=true, to_apply=%region_1.2 | all-reduce | flops 32 | bytes 256 | tf_op jit(solution)/shard_map/pmin | solution.py:85
  45.0 466.7 %while.18 = (s32[]{:T(128)}, f32[4,256]{1,0:T(4,128)S(1)}, f32[4,256]{1,0:T(4,128)S(1)}, f32[4,256,96]{1,2,0:T(8,128)S(1)}, bf16[2,256,384]{1,2,0:T(8,128)(2,1)}...) while((s32[]{:T(128)}, f32[4,256]{1,0:T(4,128)S(1)}, ...), condition=%wide.region_8.9_spmd, body=%wide.region_5.8_spmd.sunk | while | flops 103286784 | bytes 8003757 | solution.py:113
  153.3 4.9 collective-permute-start.1
  166.1 11.1 %collective-permute-start.1 = (s32[256]{0:T(256)}, s32[256]{0:T(256)S(1)}, u32[]{:S(2)}, u32[]{:S(2)}) collective-permute-start(s32[256]{0:T(256)} %get-tuple-element.160), channel_id=1, source_target_pairs={{0,8},{8,16},{16,24},{24,32},{32,40},{40,48},{48,56},{56,64},{64,7... | collective-permute-start | bytes 3080 | tf_op jit(solution)/shard_map/while/body/eval_jaxpr/ppermute | solution.py:18
  180.7 4.0 collective-permute-start
  184.7 11.4 %collective-permute-start.1 = (s32[256]{0:T(256)}, s32[256]{0:T(256)S(1)}, u32[]{:S(2)}, u32[]{:S(2)}) collective-permute-start(s32[256]{0:T(256)} %get-tuple-element.160), channel_id=1, source_target_pairs={{0,8},{8,16},{16,24},{24,32},{32,40},{40,48},{48,56},{56,64},{64,7... | collective-permute-start | bytes 3080 | tf_op jit(solution)/shard_map/while/body/eval_jaxpr/ppermute | solution.py:18
  199.5 4.0 collective-permute-start
  203.5 10.6 %collective-permute-start.1 = (s32[256]{0:T(256)}, s32[256]{0:T(256)S(1)}, u32[]{:S(2)}, u32[]{:S(2)}) collective-permute-start(s32[256]{0:T(256)} %get-tuple-element.160), channel_id=1, source_target_pairs={{0,8},{8,16},{16,24},{24,32},{32,40},{40,48},{48,56},{56,64},{64,7... | collective-permute-start | bytes 3080 | tf_op jit(solution)/shard_map/while/body/eval_jaxpr/ppermute | solution.py:18
  217.6 4.0 collective-permute-start
  221.6 9.2 %collective-permute-start.1 = (s32[256]{0:T(256)}, s32[256]{0:T(256)S(1)}, u32[]{:S(2)}, u32[]{:S(2)}) collective-permute-start(s32[256]{0:T(256)} %get-tuple-element.160), channel_id=1, source_target_pairs={{0,8},{8,16},{16,24},{24,32},{32,40},{40,48},{48,56},{56,64},{64,7... | collective-permute-start | bytes 3080 | tf_op jit(solution)/shard_map/while/body/eval_jaxpr/ppermute | solution.py:18
  234.3 4.0 collective-permute-start
  238.3 7.3 %collective-permute-start.1 = (s32[256]{0:T(256)}, s32[256]{0:T(256)S(1)}, u32[]{:S(2)}, u32[]{:S(2)}) collective-permute-start(s32[256]{0:T(256)} %get-tuple-element.160), channel_id=1, source_target_pairs={{0,8},{8,16},{16,24},{24,32},{32,40},{40,48},{48,56},{56,64},{64,7... | collective-permute-start | bytes 3080 | tf_op jit(solution)/shard_map/while/body/eval_jaxpr/ppermute | solution.py:18
  249.2 4.0 collective-permute-start
  253.2 7.3 %collective-permute-start.1 = (s32[256]{0:T(256)}, s32[256]{0:T(256)S(1)}, u32[]{:S(2)}, u32[]{:S(2)}) collective-permute-start(s32[256]{0:T(256)} %get-tuple-element.160), channel_id=1, source_target_pairs={{0,8},{8,16},{16,24},{24,32},{32,40},{40,48},{48,56},{56,64},{64,7... | collective-permute-start | bytes 3080 | tf_op jit(solution)/shard_map/while/body/eval_jaxpr/ppermute | solution.py:18
  264.0 4.0 collective-permute-start
  268.0 7.3 %collective-permute-start.1 = (s32[256]{0:T(256)}, s32[256]{0:T(256)S(1)}, u32[]{:S(2)}, u32[]{:S(2)}) collective-permute-start(s32[256]{0:T(256)} %get-tuple-element.160), channel_id=1, source_target_pairs={{0,8},{8,16},{16,24},{24,32},{32,40},{40,48},{48,56},{56,64},{64,7... | collective-permute-start | bytes 3080 | tf_op jit(solution)/shard_map/while/body/eval_jaxpr/ppermute | solution.py:18
  278.8 4.0 collective-permute-start
  282.8 7.3 %collective-permute-start.1 = (s32[256]{0:T(256)}, s32[256]{0:T(256)S(1)}, u32[]{:S(2)}, u32[]{:S(2)}) collective-permute-start(s32[256]{0:T(256)} %get-tuple-element.160), channel_id=1, source_target_pairs={{0,8},{8,16},{16,24},{24,32},{32,40},{40,48},{48,56},{56,64},{64,7... | collective-permute-start | bytes 3080 | tf_op jit(solution)/shard_map/while/body/eval_jaxpr/ppermute | solution.py:18
  293.7 4.0 collective-permute-start
  297.7 8.0 %collective-permute-start.1 = (s32[256]{0:T(256)}, s32[256]{0:T(256)S(1)}, u32[]{:S(2)}, u32[]{:S(2)}) collective-permute-start(s32[256]{0:T(256)} %get-tuple-element.160), channel_id=1, source_target_pairs={{0,8},{8,16},{16,24},{24,32},{32,40},{40,48},{48,56},{56,64},{64,7... | collective-permute-start | bytes 3080 | tf_op jit(solution)/shard_map/while/body/eval_jaxpr/ppermute | solution.py:18
  309.2 4.0 collective-permute-start
  313.3 8.0 %collective-permute-start.1 = (s32[256]{0:T(256)}, s32[256]{0:T(256)S(1)}, u32[]{:S(2)}, u32[]{:S(2)}) collective-permute-start(s32[256]{0:T(256)} %get-tuple-element.160), channel_id=1, source_target_pairs={{0,8},{8,16},{16,24},{24,32},{32,40},{40,48},{48,56},{56,64},{64,7... | collective-permute-start | bytes 3080 | tf_op jit(solution)/shard_map/while/body/eval_jaxpr/ppermute | solution.py:18
  324.8 4.0 collective-permute-start
  328.9 8.0 %collective-permute-start.1 = (s32[256]{0:T(256)}, s32[256]{0:T(256)S(1)}, u32[]{:S(2)}, u32[]{:S(2)}) collective-permute-start(s32[256]{0:T(256)} %get-tuple-element.160), channel_id=1, source_target_pairs={{0,8},{8,16},{16,24},{24,32},{32,40},{40,48},{48,56},{56,64},{64,7... | collective-permute-start | bytes 3080 | tf_op jit(solution)/shard_map/while/body/eval_jaxpr/ppermute | solution.py:18
  340.4 4.0 collective-permute-start
  344.5 8.0 %collective-permute-start.1 = (s32[256]{0:T(256)}, s32[256]{0:T(256)S(1)}, u32[]{:S(2)}, u32[]{:S(2)}) collective-permute-start(s32[256]{0:T(256)} %get-tuple-element.160), channel_id=1, source_target_pairs={{0,8},{8,16},{16,24},{24,32},{32,40},{40,48},{48,56},{56,64},{64,7... | collective-permute-start | bytes 3080 | tf_op jit(solution)/shard_map/while/body/eval_jaxpr/ppermute | solution.py:18
  356.0 4.0 collective-permute-start
  360.0 8.0 %collective-permute-start.1 = (s32[256]{0:T(256)}, s32[256]{0:T(256)S(1)}, u32[]{:S(2)}, u32[]{:S(2)}) collective-permute-start(s32[256]{0:T(256)} %get-tuple-element.160), channel_id=1, source_target_pairs={{0,8},{8,16},{16,24},{24,32},{32,40},{40,48},{48,56},{56,64},{64,7... | collective-permute-start | bytes 3080 | tf_op jit(solution)/shard_map/while/body/eval_jaxpr/ppermute | solution.py:18
  371.6 4.0 collective-permute-start
  375.6 8.0 %collective-permute-start.1 = (s32[256]{0:T(256)}, s32[256]{0:T(256)S(1)}, u32[]{:S(2)}, u32[]{:S(2)}) collective-permute-start(s32[256]{0:T(256)} %get-tuple-element.160), channel_id=1, source_target_pairs={{0,8},{8,16},{16,24},{24,32},{32,40},{40,48},{48,56},{56,64},{64,7... | collective-permute-start | bytes 3080 | tf_op jit(solution)/shard_map/while/body/eval_jaxpr/ppermute | solution.py:18
  387.1 4.0 collective-permute-start
  391.2 8.0 %collective-permute-start.1 = (s32[256]{0:T(256)}, s32[256]{0:T(256)S(1)}, u32[]{:S(2)}, u32[]{:S(2)}) collective-permute-start(s32[256]{0:T(256)} %get-tuple-element.160), channel_id=1, source_target_pairs={{0,8},{8,16},{16,24},{24,32},{32,40},{40,48},{48,56},{56,64},{64,7... | collective-permute-start | bytes 3080 | tf_op jit(solution)/shard_map/while/body/eval_jaxpr/ppermute | solution.py:18
  402.7 4.0 collective-permute-start
  406.8 8.0 %collective-permute-start.1 = (s32[256]{0:T(256)}, s32[256]{0:T(256)S(1)}, u32[]{:S(2)}, u32[]{:S(2)}) collective-permute-start(s32[256]{0:T(256)} %get-tuple-element.160), channel_id=1, source_target_pairs={{0,8},{8,16},{16,24},{24,32},{32,40},{40,48},{48,56},{56,64},{64,7... | collective-permute-start | bytes 3080 | tf_op jit(solution)/shard_map/while/body/eval_jaxpr/ppermute | solution.py:18
  418.3 4.0 collective-permute-start
  422.3 8.0 %collective-permute-start.1 = (s32[256]{0:T(256)}, s32[256]{0:T(256)S(1)}, u32[]{:S(2)}, u32[]{:S(2)}) collective-permute-start(s32[256]{0:T(256)} %get-tuple-element.160), channel_id=1, source_target_pairs={{0,8},{8,16},{16,24},{24,32},{32,40},{40,48},{48,56},{56,64},{64,7... | collective-permute-start | bytes 3080 | tf_op jit(solution)/shard_map/while/body/eval_jaxpr/ppermute | solution.py:18
  433.9 4.0 collective-permute-start
  437.9 8.0 %collective-permute-start.1 = (s32[256]{0:T(256)}, s32[256]{0:T(256)S(1)}, u32[]{:S(2)}, u32[]{:S(2)}) collective-permute-start(s32[256]{0:T(256)} %get-tuple-element.160), channel_id=1, source_target_pairs={{0,8},{8,16},{16,24},{24,32},{32,40},{40,48},{48,56},{56,64},{64,7... | collective-permute-start | bytes 3080 | tf_op jit(solution)/shard_map/while/body/eval_jaxpr/ppermute | solution.py:18
  449.5 4.0 collective-permute-start
  453.5 8.0 %collective-permute-start.1 = (s32[256]{0:T(256)}, s32[256]{0:T(256)S(1)}, u32[]{:S(2)}, u32[]{:S(2)}) collective-permute-start(s32[256]{0:T(256)} %get-tuple-element.160), channel_id=1, source_target_pairs={{0,8},{8,16},{16,24},{24,32},{32,40},{40,48},{48,56},{56,64},{64,7... | collective-permute-start | bytes 3080 | tf_op jit(solution)/shard_map/while/body/eval_jaxpr/ppermute | solution.py:18
  465.0 4.0 collective-permute-start
  469.1 8.0 %collective-permute-start.1 = (s32[256]{0:T(256)}, s32[256]{0:T(256)S(1)}, u32[]{:S(2)}, u32[]{:S(2)}) collective-permute-start(s32[256]{0:T(256)} %get-tuple-element.160), channel_id=1, source_target_pairs={{0,8},{8,16},{16,24},{24,32},{32,40},{40,48},{48,56},{56,64},{64,7... | collective-permute-start | bytes 3080 | tf_op jit(solution)/shard_map/while/body/eval_jaxpr/ppermute | solution.py:18
  480.6 4.0 collective-permute-start
  484.7 8.0 %collective-permute-start.1 = (s32[256]{0:T(256)}, s32[256]{0:T(256)S(1)}, u32[]{:S(2)}, u32[]{:S(2)}) collective-permute-start(s32[256]{0:T(256)} %get-tuple-element.160), channel_id=1, source_target_pairs={{0,8},{8,16},{16,24},{24,32},{32,40},{40,48},{48,56},{56,64},{64,7... | collective-permute-start | bytes 3080 | tf_op jit(solution)/shard_map/while/body/eval_jaxpr/ppermute | solution.py:18
  496.2 4.0 collective-permute-start
  500.2 8.0 %collective-permute-start.1 = (s32[256]{0:T(256)}, s32[256]{0:T(256)S(1)}, u32[]{:S(2)}, u32[]{:S(2)}) collective-permute-start(s32[256]{0:T(256)} %get-tuple-element.160), channel_id=1, source_target_pairs={{0,8},{8,16},{16,24},{24,32},{32,40},{40,48},{48,56},{56,64},{64,7... | collective-permute-start | bytes 3080 | tf_op jit(solution)/shard_map/while/body/eval_jaxpr/ppermute | solution.py:18
  515.4 171.0 %all-reduce.2.cloned.1.call-done = bf16[256,3072]{1,0:T(8,128)(2,1)} async-done(((bf16[256,3072]{1,0:T(8,128)(2,1)}), bf16[256,3072]{1,0:T(8,128)(2,1)}) %all-reduce.2.cloned.1.call-update) | async-done | bytes 1572880 | tf_op jit(solution)/shard_map/psum | solution.py:124
  687.5 18.4 %psum.15 = f32[256]{0:T(256)S(1)} all-reduce(f32[256]{0:T(256)S(1)} %get-tuple-element.66), channel_id=1, replica_groups=mesh['seq'=64,'tp'=8] {'tp'}, use_global_device_ids=true, to_apply=%region_11.12 | all-reduce | flops 256 | bytes 2048 | tf_op jit(solution)/shard_map/psum | solution.py:130
  (467 shorter events, 205.8 us)
Async XLA Ops:
  7.2 679.2 %all-reduce.2.cloned.1.call-start = ((), (), s32[]{:S(2)}) async-start(), calls=%async_computation | async-start | bytes 3145728 | tf_op jit(solution)/shard_map/psum | solution.py:124
  45.0 10.0 %collective-permute-start = (bf16[2,256,384]{1,2,0:T(8,128)(2,1)}, bf16[2,256,384]{1,2,0:T(8,128)(2,1)S(1)}, u32[]{:S(2)}, u32[]{:S(2)}) collective-permute-start(bf16[2,256,384]{1,2,0:T(8,128)(2,1)} %get-tuple-element.159), channel_id=1, source_target_pairs={{0,8},{8,16},{16,24},{24,32},{32,40},{40,48},{48,56},{56,64},{64,7... | collective-permute-start | bytes 1179656 | tf_op jit(solution)/shard_map/while/body/eval_jaxpr/ppermute | solution.py:18
  56.8 10.0 %collective-permute-start = (bf16[2,256,384]{1,2,0:T(8,128)(2,1)}, bf16[2,256,384]{1,2,0:T(8,128)(2,1)S(1)}, u32[]{:S(2)}, u32[]{:S(2)}) collective-permute-start(bf16[2,256,384]{1,2,0:T(8,128)(2,1)} %get-tuple-element.159), channel_id=1, source_target_pairs={{0,8},{8,16},{16,24},{24,32},{32,40},{40,48},{48,56},{56,64},{64,7... | collective-permute-start | bytes 1179656 | tf_op jit(solution)/shard_map/while/body/eval_jaxpr/ppermute | solution.py:18
  68.7 10.0 %collective-permute-start = (bf16[2,256,384]{1,2,0:T(8,128)(2,1)}, bf16[2,256,384]{1,2,0:T(8,128)(2,1)S(1)}, u32[]{:S(2)}, u32[]{:S(2)}) collective-permute-start(bf16[2,256,384]{1,2,0:T(8,128)(2,1)} %get-tuple-element.159), channel_id=1, source_target_pairs={{0,8},{8,16},{16,24},{24,32},{32,40},{40,48},{48,56},{56,64},{64,7... | collective-permute-start | bytes 1179656 | tf_op jit(solution)/shard_map/while/body/eval_jaxpr/ppermute | solution.py:18
  80.5 10.0 %collective-permute-start = (bf16[2,256,384]{1,2,0:T(8,128)(2,1)}, bf16[2,256,384]{1,2,0:T(8,128)(2,1)S(1)}, u32[]{:S(2)}, u32[]{:S(2)}) collective-permute-start(bf16[2,256,384]{1,2,0:T(8,128)(2,1)} %get-tuple-element.159), channel_id=1, source_target_pairs={{0,8},{8,16},{16,24},{24,32},{32,40},{40,48},{48,56},{56,64},{64,7... | collective-permute-start | bytes 1179656 | tf_op jit(solution)/shard_map/while/body/eval_jaxpr/ppermute | solution.py:18
  92.3 10.0 %collective-permute-start = (bf16[2,256,384]{1,2,0:T(8,128)(2,1)}, bf16[2,256,384]{1,2,0:T(8,128)(2,1)S(1)}, u32[]{:S(2)}, u32[]{:S(2)}) collective-permute-start(bf16[2,256,384]{1,2,0:T(8,128)(2,1)} %get-tuple-element.159), channel_id=1, source_target_pairs={{0,8},{8,16},{16,24},{24,32},{32,40},{40,48},{48,56},{56,64},{64,7... | collective-permute-start | bytes 1179656 | tf_op jit(solution)/shard_map/while/body/eval_jaxpr/ppermute | solution.py:18
  104.1 10.0 %collective-permute-start = (bf16[2,256,384]{1,2,0:T(8,128)(2,1)}, bf16[2,256,384]{1,2,0:T(8,128)(2,1)S(1)}, u32[]{:S(2)}, u32[]{:S(2)}) collective-permute-start(bf16[2,256,384]{1,2,0:T(8,128)(2,1)} %get-tuple-element.159), channel_id=1, source_target_pairs={{0,8},{8,16},{16,24},{24,32},{32,40},{40,48},{48,56},{56,64},{64,7... | collective-permute-start | bytes 1179656 | tf_op jit(solution)/shard_map/while/body/eval_jaxpr/ppermute | solution.py:18
  116.0 10.0 %collective-permute-start = (bf16[2,256,384]{1,2,0:T(8,128)(2,1)}, bf16[2,256,384]{1,2,0:T(8,128)(2,1)S(1)}, u32[]{:S(2)}, u32[]{:S(2)}) collective-permute-start(bf16[2,256,384]{1,2,0:T(8,128)(2,1)} %get-tuple-element.159), channel_id=1, source_target_pairs={{0,8},{8,16},{16,24},{24,32},{32,40},{40,48},{48,56},{56,64},{64,7... | collective-permute-start | bytes 1179656 | tf_op jit(solution)/shard_map/while/body/eval_jaxpr/ppermute | solution.py:18
  127.8 10.0 %collective-permute-start = (bf16[2,256,384]{1,2,0:T(8,128)(2,1)}, bf16[2,256,384]{1,2,0:T(8,128)(2,1)S(1)}, u32[]{:S(2)}, u32[]{:S(2)}) collective-permute-start(bf16[2,256,384]{1,2,0:T(8,128)(2,1)} %get-tuple-element.159), channel_id=1, source_target_pairs={{0,8},{8,16},{16,24},{24,32},{32,40},{40,48},{48,56},{56,64},{64,7... | collective-permute-start | bytes 1179656 | tf_op jit(solution)/shard_map/while/body/eval_jaxpr/ppermute | solution.py:18
  139.6 10.0 %collective-permute-start = (bf16[2,256,384]{1,2,0:T(8,128)(2,1)}, bf16[2,256,384]{1,2,0:T(8,128)(2,1)S(1)}, u32[]{:S(2)}, u32[]{:S(2)}) collective-permute-start(bf16[2,256,384]{1,2,0:T(8,128)(2,1)} %get-tuple-element.159), channel_id=1, source_target_pairs={{0,8},{8,16},{16,24},{24,32},{32,40},{40,48},{48,56},{56,64},{64,7... | collective-permute-start | bytes 1179656 | tf_op jit(solution)/shard_map/while/body/eval_jaxpr/ppermute | solution.py:18
  151.4 10.0 %collective-permute-start = (bf16[2,256,384]{1,2,0:T(8,128)(2,1)}, bf16[2,256,384]{1,2,0:T(8,128)(2,1)S(1)}, u32[]{:S(2)}, u32[]{:S(2)}) collective-permute-start(bf16[2,256,384]{1,2,0:T(8,128)(2,1)} %get-tuple-element.159), channel_id=1, source_target_pairs={{0,8},{8,16},{16,24},{24,32},{32,40},{40,48},{48,56},{56,64},{64,7... | collective-permute-start | bytes 1179656 | tf_op jit(solution)/shard_map/while/body/eval_jaxpr/ppermute | solution.py:18
  163.3 15.6 %collective-permute-start = (bf16[2,256,384]{1,2,0:T(8,128)(2,1)}, bf16[2,256,384]{1,2,0:T(8,128)(2,1)S(1)}, u32[]{:S(2)}, u32[]{:S(2)}) collective-permute-start(bf16[2,256,384]{1,2,0:T(8,128)(2,1)} %get-tuple-element.159), channel_id=1, source_target_pairs={{0,8},{8,16},{16,24},{24,32},{32,40},{40,48},{48,56},{56,64},{64,7... | collective-permute-start | bytes 1179656 | tf_op jit(solution)/shard_map/while/body/eval_jaxpr/ppermute | solution.py:18
  166.1 12.1 %collective-permute-start.1 = (s32[256]{0:T(256)}, s32[256]{0:T(256)S(1)}, u32[]{:S(2)}, u32[]{:S(2)}) collective-permute-start(s32[256]{0:T(256)} %get-tuple-element.160), channel_id=1, source_target_pairs={{0,8},{8,16},{16,24},{24,32},{32,40},{40,48},{48,56},{56,64},{64,7... | collective-permute-start | bytes 3080 | tf_op jit(solution)/shard_map/while/body/eval_jaxpr/ppermute | solution.py:18
  180.7 17.1 %collective-permute-start = (bf16[2,256,384]{1,2,0:T(8,128)(2,1)}, bf16[2,256,384]{1,2,0:T(8,128)(2,1)S(1)}, u32[]{:S(2)}, u32[]{:S(2)}) collective-permute-start(bf16[2,256,384]{1,2,0:T(8,128)(2,1)} %get-tuple-element.159), channel_id=1, source_target_pairs={{0,8},{8,16},{16,24},{24,32},{32,40},{40,48},{48,56},{56,64},{64,7... | collective-permute-start | bytes 1179656 | tf_op jit(solution)/shard_map/while/body/eval_jaxpr/ppermute | solution.py:18
  184.7 12.4 %collective-permute-start.1 = (s32[256]{0:T(256)}, s32[256]{0:T(256)S(1)}, u32[]{:S(2)}, u32[]{:S(2)}) collective-permute-start(s32[256]{0:T(256)} %get-tuple-element.160), channel_id=1, source_target_pairs={{0,8},{8,16},{16,24},{24,32},{32,40},{40,48},{48,56},{56,64},{64,7... | collective-permute-start | bytes 3080 | tf_op jit(solution)/shard_map/while/body/eval_jaxpr/ppermute | solution.py:18
  199.5 16.3 %collective-permute-start = (bf16[2,256,384]{1,2,0:T(8,128)(2,1)}, bf16[2,256,384]{1,2,0:T(8,128)(2,1)S(1)}, u32[]{:S(2)}, u32[]{:S(2)}) collective-permute-start(bf16[2,256,384]{1,2,0:T(8,128)(2,1)} %get-tuple-element.159), channel_id=1, source_target_pairs={{0,8},{8,16},{16,24},{24,32},{32,40},{40,48},{48,56},{56,64},{64,7... | collective-permute-start | bytes 1179656 | tf_op jit(solution)/shard_map/while/body/eval_jaxpr/ppermute | solution.py:18
  203.5 11.6 %collective-permute-start.1 = (s32[256]{0:T(256)}, s32[256]{0:T(256)S(1)}, u32[]{:S(2)}, u32[]{:S(2)}) collective-permute-start(s32[256]{0:T(256)} %get-tuple-element.160), channel_id=1, source_target_pairs={{0,8},{8,16},{16,24},{24,32},{32,40},{40,48},{48,56},{56,64},{64,7... | collective-permute-start | bytes 3080 | tf_op jit(solution)/shard_map/while/body/eval_jaxpr/ppermute | solution.py:18
  217.6 14.9 %collective-permute-start = (bf16[2,256,384]{1,2,0:T(8,128)(2,1)}, bf16[2,256,384]{1,2,0:T(8,128)(2,1)S(1)}, u32[]{:S(2)}, u32[]{:S(2)}) collective-permute-start(bf16[2,256,384]{1,2,0:T(8,128)(2,1)} %get-tuple-element.159), channel_id=1, source_target_pairs={{0,8},{8,16},{16,24},{24,32},{32,40},{40,48},{48,56},{56,64},{64,7... | collective-permute-start | bytes 1179656 | tf_op jit(solution)/shard_map/while/body/eval_jaxpr/ppermute | solution.py:18
  221.6 10.2 %collective-permute-start.1 = (s32[256]{0:T(256)}, s32[256]{0:T(256)S(1)}, u32[]{:S(2)}, u32[]{:S(2)}) collective-permute-start(s32[256]{0:T(256)} %get-tuple-element.160), channel_id=1, source_target_pairs={{0,8},{8,16},{16,24},{24,32},{32,40},{40,48},{48,56},{56,64},{64,7... | collective-permute-start | bytes 3080 | tf_op jit(solution)/shard_map/while/body/eval_jaxpr/ppermute | solution.py:18
  234.3 13.0 %collective-permute-start = (bf16[2,256,384]{1,2,0:T(8,128)(2,1)}, bf16[2,256,384]{1,2,0:T(8,128)(2,1)S(1)}, u32[]{:S(2)}, u32[]{:S(2)}) collective-permute-start(bf16[2,256,384]{1,2,0:T(8,128)(2,1)} %get-tuple-element.159), channel_id=1, source_target_pairs={{0,8},{8,16},{16,24},{24,32},{32,40},{40,48},{48,56},{56,64},{64,7... | collective-permute-start | bytes 1179656 | tf_op jit(solution)/shard_map/while/body/eval_jaxpr/ppermute | solution.py:18
  249.2 13.0 %collective-permute-start = (bf16[2,256,384]{1,2,0:T(8,128)(2,1)}, bf16[2,256,384]{1,2,0:T(8,128)(2,1)S(1)}, u32[]{:S(2)}, u32[]{:S(2)}) collective-permute-start(bf16[2,256,384]{1,2,0:T(8,128)(2,1)} %get-tuple-element.159), channel_id=1, source_target_pairs={{0,8},{8,16},{16,24},{24,32},{32,40},{40,48},{48,56},{56,64},{64,7... | collective-permute-start | bytes 1179656 | tf_op jit(solution)/shard_map/while/body/eval_jaxpr/ppermute | solution.py:18
  264.0 13.0 %collective-permute-start = (bf16[2,256,384]{1,2,0:T(8,128)(2,1)}, bf16[2,256,384]{1,2,0:T(8,128)(2,1)S(1)}, u32[]{:S(2)}, u32[]{:S(2)}) collective-permute-start(bf16[2,256,384]{1,2,0:T(8,128)(2,1)} %get-tuple-element.159), channel_id=1, source_target_pairs={{0,8},{8,16},{16,24},{24,32},{32,40},{40,48},{48,56},{56,64},{64,7... | collective-permute-start | bytes 1179656 | tf_op jit(solution)/shard_map/while/body/eval_jaxpr/ppermute | solution.py:18
  278.8 13.0 %collective-permute-start = (bf16[2,256,384]{1,2,0:T(8,128)(2,1)}, bf16[2,256,384]{1,2,0:T(8,128)(2,1)S(1)}, u32[]{:S(2)}, u32[]{:S(2)}) collective-permute-start(bf16[2,256,384]{1,2,0:T(8,128)(2,1)} %get-tuple-element.159), channel_id=1, source_target_pairs={{0,8},{8,16},{16,24},{24,32},{32,40},{40,48},{48,56},{56,64},{64,7... | collective-permute-start | bytes 1179656 | tf_op jit(solution)/shard_map/while/body/eval_jaxpr/ppermute | solution.py:18
  293.7 13.8 %collective-permute-start = (bf16[2,256,384]{1,2,0:T(8,128)(2,1)}, bf16[2,256,384]{1,2,0:T(8,128)(2,1)S(1)}, u32[]{:S(2)}, u32[]{:S(2)}) collective-permute-start(bf16[2,256,384]{1,2,0:T(8,128)(2,1)} %get-tuple-element.159), channel_id=1, source_target_pairs={{0,8},{8,16},{16,24},{24,32},{32,40},{40,48},{48,56},{56,64},{64,7... | collective-permute-start | bytes 1179656 | tf_op jit(solution)/shard_map/while/body/eval_jaxpr/ppermute | solution.py:18
  297.7 9.1 %collective-permute-start.1 = (s32[256]{0:T(256)}, s32[256]{0:T(256)S(1)}, u32[]{:S(2)}, u32[]{:S(2)}) collective-permute-start(s32[256]{0:T(256)} %get-tuple-element.160), channel_id=1, source_target_pairs={{0,8},{8,16},{16,24},{24,32},{32,40},{40,48},{48,56},{56,64},{64,7... | collective-permute-start | bytes 3080 | tf_op jit(solution)/shard_map/while/body/eval_jaxpr/ppermute | solution.py:18
  309.2 13.8 %collective-permute-start = (bf16[2,256,384]{1,2,0:T(8,128)(2,1)}, bf16[2,256,384]{1,2,0:T(8,128)(2,1)S(1)}, u32[]{:S(2)}, u32[]{:S(2)}) collective-permute-start(bf16[2,256,384]{1,2,0:T(8,128)(2,1)} %get-tuple-element.159), channel_id=1, source_target_pairs={{0,8},{8,16},{16,24},{24,32},{32,40},{40,48},{48,56},{56,64},{64,7... | collective-permute-start | bytes 1179656 | tf_op jit(solution)/shard_map/while/body/eval_jaxpr/ppermute | solution.py:18
  313.3 9.1 %collective-permute-start.1 = (s32[256]{0:T(256)}, s32[256]{0:T(256)S(1)}, u32[]{:S(2)}, u32[]{:S(2)}) collective-permute-start(s32[256]{0:T(256)} %get-tuple-element.160), channel_id=1, source_target_pairs={{0,8},{8,16},{16,24},{24,32},{32,40},{40,48},{48,56},{56,64},{64,7... | collective-permute-start | bytes 3080 | tf_op jit(solution)/shard_map/while/body/eval_jaxpr/ppermute | solution.py:18
  324.8 13.8 %collective-permute-start = (bf16[2,256,384]{1,2,0:T(8,128)(2,1)}, bf16[2,256,384]{1,2,0:T(8,128)(2,1)S(1)}, u32[]{:S(2)}, u32[]{:S(2)}) collective-permute-start(bf16[2,256,384]{1,2,0:T(8,128)(2,1)} %get-tuple-element.159), channel_id=1, source_target_pairs={{0,8},{8,16},{16,24},{24,32},{32,40},{40,48},{48,56},{56,64},{64,7... | collective-permute-start | bytes 1179656 | tf_op jit(solution)/shard_map/while/body/eval_jaxpr/ppermute | solution.py:18
  328.9 9.1 %collective-permute-start.1 = (s32[256]{0:T(256)}, s32[256]{0:T(256)S(1)}, u32[]{:S(2)}, u32[]{:S(2)}) collective-permute-start(s32[256]{0:T(256)} %get-tuple-element.160), channel_id=1, source_target_pairs={{0,8},{8,16},{16,24},{24,32},{32,40},{40,48},{48,56},{56,64},{64,7... | collective-permute-start | bytes 3080 | tf_op jit(solution)/shard_map/while/body/eval_jaxpr/ppermute | solution.py:18
  340.4 13.8 %collective-permute-start = (bf16[2,256,384]{1,2,0:T(8,128)(2,1)}, bf16[2,256,384]{1,2,0:T(8,128)(2,1)S(1)}, u32[]{:S(2)}, u32[]{:S(2)}) collective-permute-start(bf16[2,256,384]{1,2,0:T(8,128)(2,1)} %get-tuple-element.159), channel_id=1, source_target_pairs={{0,8},{8,16},{16,24},{24,32},{32,40},{40,48},{48,56},{56,64},{64,7... | collective-permute-start | bytes 1179656 | tf_op jit(solution)/shard_map/while/body/eval_jaxpr/ppermute | solution.py:18
  344.5 9.1 %collective-permute-start.1 = (s32[256]{0:T(256)}, s32[256]{0:T(256)S(1)}, u32[]{:S(2)}, u32[]{:S(2)}) collective-permute-start(s32[256]{0:T(256)} %get-tuple-element.160), channel_id=1, source_target_pairs={{0,8},{8,16},{16,24},{24,32},{32,40},{40,48},{48,56},{56,64},{64,7... | collective-permute-start | bytes 3080 | tf_op jit(solution)/shard_map/while/body/eval_jaxpr/ppermute | solution.py:18
  356.0 13.8 %collective-permute-start = (bf16[2,256,384]{1,2,0:T(8,128)(2,1)}, bf16[2,256,384]{1,2,0:T(8,128)(2,1)S(1)}, u32[]{:S(2)}, u32[]{:S(2)}) collective-permute-start(bf16[2,256,384]{1,2,0:T(8,128)(2,1)} %get-tuple-element.159), channel_id=1, source_target_pairs={{0,8},{8,16},{16,24},{24,32},{32,40},{40,48},{48,56},{56,64},{64,7... | collective-permute-start | bytes 1179656 | tf_op jit(solution)/shard_map/while/body/eval_jaxpr/ppermute | solution.py:18
  360.0 9.1 %collective-permute-start.1 = (s32[256]{0:T(256)}, s32[256]{0:T(256)S(1)}, u32[]{:S(2)}, u32[]{:S(2)}) collective-permute-start(s32[256]{0:T(256)} %get-tuple-element.160), channel_id=1, source_target_pairs={{0,8},{8,16},{16,24},{24,32},{32,40},{40,48},{48,56},{56,64},{64,7... | collective-permute-start | bytes 3080 | tf_op jit(solution)/shard_map/while/body/eval_jaxpr/ppermute | solution.py:18
  371.6 13.8 %collective-permute-start = (bf16[2,256,384]{1,2,0:T(8,128)(2,1)}, bf16[2,256,384]{1,2,0:T(8,128)(2,1)S(1)}, u32[]{:S(2)}, u32[]{:S(2)}) collective-permute-start(bf16[2,256,384]{1,2,0:T(8,128)(2,1)} %get-tuple-element.159), channel_id=1, source_target_pairs={{0,8},{8,16},{16,24},{24,32},{32,40},{40,48},{48,56},{56,64},{64,7... | collective-permute-start | bytes 1179656 | tf_op jit(solution)/shard_map/while/body/eval_jaxpr/ppermute | solution.py:18
  375.6 9.1 %collective-permute-start.1 = (s32[256]{0:T(256)}, s32[256]{0:T(256)S(1)}, u32[]{:S(2)}, u32[]{:S(2)}) collective-permute-start(s32[256]{0:T(256)} %get-tuple-element.160), channel_id=1, source_target_pairs={{0,8},{8,16},{16,24},{24,32},{32,40},{40,48},{48,56},{56,64},{64,7... | collective-permute-start | bytes 3080 | tf_op jit(solution)/shard_map/while/body/eval_jaxpr/ppermute | solution.py:18
  387.1 13.8 %collective-permute-start = (bf16[2,256,384]{1,2,0:T(8,128)(2,1)}, bf16[2,256,384]{1,2,0:T(8,128)(2,1)S(1)}, u32[]{:S(2)}, u32[]{:S(2)}) collective-permute-start(bf16[2,256,384]{1,2,0:T(8,128)(2,1)} %get-tuple-element.159), channel_id=1, source_target_pairs={{0,8},{8,16},{16,24},{24,32},{32,40},{40,48},{48,56},{56,64},{64,7... | collective-permute-start | bytes 1179656 | tf_op jit(solution)/shard_map/while/body/eval_jaxpr/ppermute | solution.py:18
  391.2 9.1 %collective-permute-start.1 = (s32[256]{0:T(256)}, s32[256]{0:T(256)S(1)}, u32[]{:S(2)}, u32[]{:S(2)}) collective-permute-start(s32[256]{0:T(256)} %get-tuple-element.160), channel_id=1, source_target_pairs={{0,8},{8,16},{16,24},{24,32},{32,40},{40,48},{48,56},{56,64},{64,7... | collective-permute-start | bytes 3080 | tf_op jit(solution)/shard_map/while/body/eval_jaxpr/ppermute | solution.py:18
  402.7 13.8 %collective-permute-start = (bf16[2,256,384]{1,2,0:T(8,128)(2,1)}, bf16[2,256,384]{1,2,0:T(8,128)(2,1)S(1)}, u32[]{:S(2)}, u32[]{:S(2)}) collective-permute-start(bf16[2,256,384]{1,2,0:T(8,128)(2,1)} %get-tuple-element.159), channel_id=1, source_target_pairs={{0,8},{8,16},{16,24},{24,32},{32,40},{40,48},{48,56},{56,64},{64,7... | collective-permute-start | bytes 1179656 | tf_op jit(solution)/shard_map/while/body/eval_jaxpr/ppermute | solution.py:18
  406.8 9.1 %collective-permute-start.1 = (s32[256]{0:T(256)}, s32[256]{0:T(256)S(1)}, u32[]{:S(2)}, u32[]{:S(2)}) collective-permute-start(s32[256]{0:T(256)} %get-tuple-element.160), channel_id=1, source_target_pairs={{0,8},{8,16},{16,24},{24,32},{32,40},{40,48},{48,56},{56,64},{64,7... | collective-permute-start | bytes 3080 | tf_op jit(solution)/shard_map/while/body/eval_jaxpr/ppermute | solution.py:18
  418.3 13.8 %collective-permute-start = (bf16[2,256,384]{1,2,0:T(8,128)(2,1)}, bf16[2,256,384]{1,2,0:T(8,128)(2,1)S(1)}, u32[]{:S(2)}, u32[]{:S(2)}) collective-permute-start(bf16[2,256,384]{1,2,0:T(8,128)(2,1)} %get-tuple-element.159), channel_id=1, source_target_pairs={{0,8},{8,16},{16,24},{24,32},{32,40},{40,48},{48,56},{56,64},{64,7... | collective-permute-start | bytes 1179656 | tf_op jit(solution)/shard_map/while/body/eval_jaxpr/ppermute | solution.py:18
  422.3 9.1 %collective-permute-start.1 = (s32[256]{0:T(256)}, s32[256]{0:T(256)S(1)}, u32[]{:S(2)}, u32[]{:S(2)}) collective-permute-start(s32[256]{0:T(256)} %get-tuple-element.160), channel_id=1, source_target_pairs={{0,8},{8,16},{16,24},{24,32},{32,40},{40,48},{48,56},{56,64},{64,7... | collective-permute-start | bytes 3080 | tf_op jit(solution)/shard_map/while/body/eval_jaxpr/ppermute | solution.py:18
  433.9 13.8 %collective-permute-start = (bf16[2,256,384]{1,2,0:T(8,128)(2,1)}, bf16[2,256,384]{1,2,0:T(8,128)(2,1)S(1)}, u32[]{:S(2)}, u32[]{:S(2)}) collective-permute-start(bf16[2,256,384]{1,2,0:T(8,128)(2,1)} %get-tuple-element.159), channel_id=1, source_target_pairs={{0,8},{8,16},{16,24},{24,32},{32,40},{40,48},{48,56},{56,64},{64,7... | collective-permute-start | bytes 1179656 | tf_op jit(solution)/shard_map/while/body/eval_jaxpr/ppermute | solution.py:18
  449.5 13.8 %collective-permute-start = (bf16[2,256,384]{1,2,0:T(8,128)(2,1)}, bf16[2,256,384]{1,2,0:T(8,128)(2,1)S(1)}, u32[]{:S(2)}, u32[]{:S(2)}) collective-permute-start(bf16[2,256,384]{1,2,0:T(8,128)(2,1)} %get-tuple-element.159), channel_id=1, source_target_pairs={{0,8},{8,16},{16,24},{24,32},{32,40},{40,48},{48,56},{56,64},{64,7... | collective-permute-start | bytes 1179656 | tf_op jit(solution)/shard_map/while/body/eval_jaxpr/ppermute | solution.py:18
  453.5 9.1 %collective-permute-start.1 = (s32[256]{0:T(256)}, s32[256]{0:T(256)S(1)}, u32[]{:S(2)}, u32[]{:S(2)}) collective-permute-start(s32[256]{0:T(256)} %get-tuple-element.160), channel_id=1, source_target_pairs={{0,8},{8,16},{16,24},{24,32},{32,40},{40,48},{48,56},{56,64},{64,7... | collective-permute-start | bytes 3080 | tf_op jit(solution)/shard_map/while/body/eval_jaxpr/ppermute | solution.py:18
  465.0 13.8 %collective-permute-start = (bf16[2,256,384]{1,2,0:T(8,128)(2,1)}, bf16[2,256,384]{1,2,0:T(8,128)(2,1)S(1)}, u32[]{:S(2)}, u32[]{:S(2)}) collective-permute-start(bf16[2,256,384]{1,2,0:T(8,128)(2,1)} %get-tuple-element.159), channel_id=1, source_target_pairs={{0,8},{8,16},{16,24},{24,32},{32,40},{40,48},{48,56},{56,64},{64,7... | collective-permute-start | bytes 1179656 | tf_op jit(solution)/shard_map/while/body/eval_jaxpr/ppermute | solution.py:18
  480.6 13.8 %collective-permute-start = (bf16[2,256,384]{1,2,0:T(8,128)(2,1)}, bf16[2,256,384]{1,2,0:T(8,128)(2,1)S(1)}, u32[]{:S(2)}, u32[]{:S(2)}) collective-permute-start(bf16[2,256,384]{1,2,0:T(8,128)(2,1)} %get-tuple-element.159), channel_id=1, source_target_pairs={{0,8},{8,16},{16,24},{24,32},{32,40},{40,48},{48,56},{56,64},{64,7... | collective-permute-start | bytes 1179656 | tf_op jit(solution)/shard_map/while/body/eval_jaxpr/ppermute | solution.py:18
  496.2 13.8 %collective-permute-start = (bf16[2,256,384]{1,2,0:T(8,128)(2,1)}, bf16[2,256,384]{1,2,0:T(8,128)(2,1)S(1)}, u32[]{:S(2)}, u32[]{:S(2)}) collective-permute-start(bf16[2,256,384]{1,2,0:T(8,128)(2,1)} %get-tuple-element.159), channel_id=1, source_target_pairs={{0,8},{8,16},{16,24},{24,32},{32,40},{40,48},{48,56},{56,64},{64,7... | collective-permute-start | bytes 1179656 | tf_op jit(solution)/shard_map/while/body/eval_jaxpr/ppermute | solution.py:18
  500.2 9.1 %collective-permute-start.1 = (s32[256]{0:T(256)}, s32[256]{0:T(256)S(1)}, u32[]{:S(2)}, u32[]{:S(2)}) collective-permute-start(s32[256]{0:T(256)} %get-tuple-element.160), channel_id=1, source_target_pairs={{0,8},{8,16},{16,24},{24,32},{32,40},{40,48},{48,56},{56,64},{64,7... | collective-permute-start | bytes 3080 | tf_op jit(solution)/shard_map/while/body/eval_jaxpr/ppermute | solution.py:18
  (30 other events, 1099.8 us)
Sparse Core Ops, SparseCore 0:
  514.2 172.1 all-reduce.1
where the time goes:
time: 716 us; the launch traced here: 713 us
  starting transfers between devices  327 us (46%)
  waiting for transfers between devices  231 us (32%)
  local copies, waits for them, and re-layouts  47.7 us (7%)
  blocking collectives  46.6 us (7%)
  matrix products  28 us (4%)
  other arithmetic  16.5 us (2%)
  between operations  14.3 us (2%)
    ppermute x64, starting transfers between devices, passed_along(): return lax.ppermute(block, axis, route)  327 us
    psum x1, waiting for transfers between devices, per_device(): lax.psum(partial_value.astype(jnp.bfloat16), 'tp').astype(jnp.float32)  171 us
    ppermute x64, waiting for transfers between devices, passed_along(): return lax.ppermute(block, axis, route)  59.6 us
    while x96, local copies, waits for them, and re-layouts  42 us
    pmin x1, blocking collectives, per_device(): first_tok = lax.pmin(local_first, 'seq')  28.3 us
    psum x1, blocking collectives, per_device(): square_total = lax.psum(jnp.sum(stream_wide * stream_wide, axis=1), 'tp')  18.4 us
  transfers between devices with their start and end apart: 65, of which 33 were waited for; matrix products, arithmetic and copies ran while one was open for 3% of the time, Pallas kernels for 0%

commit v1 on v0

--- a/solution.py
+++ b/solution.py
@@ -121,7 +121,9 @@
     )
     partial_value = jnp.dot(attn, out_weight, preferred_element_type=jnp.float32)
     feature_width = hidden.shape[1]
-    summed = lax.psum(partial_value.astype(jnp.bfloat16), "tp").astype(jnp.float32)
+    summed = jnp.sum(lax.all_gather(partial_value.astype(jnp.bfloat16), "tp"), axis=0).astype(
+        jnp.float32
+    )
     own_sum = lax.dynamic_slice_in_dim(
         summed, lax.axis_index("tp") * feature_width, feature_width, 1
     )

time: 716 us -> 879 us (1.23)
  waiting for transfers between devices: 231 us -> 385 us
  other arithmetic: 16.5 us -> 25.4 us
    all_gather x0 -> x1, waiting for transfers between devices: none -> 326 us  [per_device(): lax.all_gather(partial_value.astype(jnp.bfloat16), 'tp')]
    psum x1 -> x0, waiting for transfers between devices: 171 us -> none  [per_device(): lax.psum(partial_value.astype(jnp.bfloat16), 'tp').astype(jnp.float32)]
where the time goes in v1:
time: 879 us; the launch traced here: 876 us
  waiting for transfers between devices  385 us (44%)
  starting transfers between devices  327 us (37%)
  local copies, waits for them, and re-layouts  47.7 us (5%)
  blocking collectives  46.8 us (5%)
  matrix products  28.1 us (3%)
  other arithmetic  25.4 us (3%)
  between operations  14.3 us (2%)
    ppermute x64, starting transfers between devices, passed_along(): return lax.ppermute(block, axis, route)  326 us
    all_gather x1, waiting for transfers between devices, per_device(): lax.all_gather(partial_value.astype(jnp.bfloat16), 'tp')  326 us
    ppermute x64, waiting for transfers between devices, passed_along(): return lax.ppermute(block, axis, route)  59.6 us
    while x96, local copies, waits for them, and re-layouts  42 us
    pmin x1, blocking collectives, per_device(): first_tok = lax.pmin(local_first, 'seq')  28.3 us
    psum x1, blocking collectives, per_device(): square_total = lax.psum(jnp.sum(stream_wide * stream_wide, axis=1), 'tp')  18.5 us
  transfers between devices with their start and end apart: 65, of which 33 were waited for; matrix products, arithmetic and copies ran while one was open for 3% of the time, Pallas kernels for 0%

profile of v1, /device:TPU:8, one launch (start us, length us, event | category | flops | bytes accessed | tf_op | source)
XLA Modules:
  0.0 876.4 jit_solution(2473615842424118880)
XLA Ops:
  8.2 28.3 %pmin.7 = s32[32]{0:T(128)S(1)} all-reduce(s32[32]{0:T(128)S(1)} %select_reduce_fusion.1), channel_id=1, replica_groups=mesh['seq'=64,'tp'=8] {'seq'}, use_global_device_ids=true, to_apply=%region_1.2 | all-reduce | flops 32 | bytes 256 | tf_op jit(solution)/shard_map/pmin | solution.py:85
  45.1 465.9 %while.18 = (s32[]{:T(128)}, f32[4,256]{1,0:T(4,128)S(1)}, f32[4,256]{1,0:T(4,128)S(1)}, f32[4,256,96]{1,2,0:T(8,128)S(1)}, bf16[2,256,384]{1,2,0:T(8,128)(2,1)}...) while((s32[]{:T(128)}, f32[4,256]{1,0:T(4,128)S(1)}, ...), condition=%wide.region_8.9_spmd, body=%wide.region_5.8_spmd.sunk | while | flops 103286784 | bytes 8003757 | solution.py:113
  153.4 4.9 collective-permute-start.1
  166.1 11.1 %collective-permute-start.1 = (s32[256]{0:T(256)}, s32[256]{0:T(256)S(1)}, u32[]{:S(2)}, u32[]{:S(2)}) collective-permute-start(s32[256]{0:T(256)} %get-tuple-element.160), channel_id=1, source_target_pairs={{0,8},{8,16},{16,24},{24,32},{32,40},{40,48},{48,56},{56,64},{64,7... | collective-permute-start | bytes 3080 | tf_op jit(solution)/shard_map/while/body/eval_jaxpr/ppermute | solution.py:18
  180.7 4.0 collective-permute-start
  184.7 11.4 %collective-permute-start.1 = (s32[256]{0:T(256)}, s32[256]{0:T(256)S(1)}, u32[]{:S(2)}, u32[]{:S(2)}) collective-permute-start(s32[256]{0:T(256)} %get-tuple-element.160), channel_id=1, source_target_pairs={{0,8},{8,16},{16,24},{24,32},{32,40},{40,48},{48,56},{56,64},{64,7... | collective-permute-start | bytes 3080 | tf_op jit(solution)/shard_map/while/body/eval_jaxpr/ppermute | solution.py:18
  199.6 4.0 collective-permute-start
  203.6 10.6 %collective-permute-start.1 = (s32[256]{0:T(256)}, s32[256]{0:T(256)S(1)}, u32[]{:S(2)}, u32[]{:S(2)}) collective-permute-start(s32[256]{0:T(256)} %get-tuple-element.160), channel_id=1, source_target_pairs={{0,8},{8,16},{16,24},{24,32},{32,40},{40,48},{48,56},{56,64},{64,7... | collective-permute-start | bytes 3080 | tf_op jit(solution)/shard_map/while/body/eval_jaxpr/ppermute | solution.py:18
  217.7 4.0 collective-permute-start
  221.7 9.3 %collective-permute-start.1 = (s32[256]{0:T(256)}, s32[256]{0:T(256)S(1)}, u32[]{:S(2)}, u32[]{:S(2)}) collective-permute-start(s32[256]{0:T(256)} %get-tuple-element.160), channel_id=1, source_target_pairs={{0,8},{8,16},{16,24},{24,32},{32,40},{40,48},{48,56},{56,64},{64,7... | collective-permute-start | bytes 3080 | tf_op jit(solution)/shard_map/while/body/eval_jaxpr/ppermute | solution.py:18
  234.4 4.0 collective-permute-start
  238.4 7.3 collective-permute-start.1
  249.3 4.0 collective-permute-start
  253.3 7.3 collective-permute-start.1
  264.1 4.0 collective-permute-start
  268.1 7.3 collective-permute-start.1
  278.9 4.0 collective-permute-start
  282.9 7.3 collective-permute-start.1
  293.8 4.0 collective-permute-start
  297.8 8.0 collective-permute-start.1
  309.3 4.0 collective-permute-start
  313.3 8.0 collective-permute-start.1
  324.9 4.0 collective-permute-start
  328.9 8.0 collective-permute-start.1
  340.4 4.0 collective-permute-start
  344.4 8.0 collective-permute-start.1
  355.9 4.0 collective-permute-start
  359.9 8.0 collective-permute-start.1
  371.4 4.0 collective-permute-start
  375.4 8.0 collective-permute-start.1
  390.9 8.0 collective-permute-start.1
  402.5 4.0 collective-permute-start
  406.4 8.0 collective-permute-start.1
  418.0 4.0 collective-permute-start
  422.0 8.0 collective-permute-start.1
  433.5 4.0 collective-permute-start
  437.5 8.0 collective-permute-start.1
  449.0 4.0 collective-permute-start
  453.0 8.0 collective-permute-start.1
  464.5 4.0 collective-permute-start
  468.5 8.0 collective-permute-start.1
  480.0 4.0 collective-permute-start
  484.0 8.0 collective-permute-start.1
  495.5 4.0 collective-permute-start
  499.5 8.0 collective-permute-start.1
  514.7 325.7 %all-gather.3.cloned.1.call-done = bf16[2048,3072]{1,0:T(8,128)(2,1)} async-done(((bf16[256,3072]{1,0:T(8,128)(2,1)}), bf16[2048,3072]{1,0:T(8,128)(2,1)}) %all-gather.3.cloned.1.call-update) | async-done | bytes 12582928 | tf_op jit(solution)/shard_map/all_gather | solution.py:124
  840.3 8.8 %reduce_sum.50 = bf16[256,3072]{1,0:T(8,128)(2,1)} reduce(bf16[8,256,3072]{2,1,0:T(8,128)(2,1)} %bitcast.37, bf16[]{:T(256)} %constant.16.clone.1), dimensions={0}, to_apply=%region_9.10 | reduce | flops 5505024 | bytes 14155778 | tf_op jit(solution)/shard_map/reduce_sum | solution.py:124
  850.2 18.5 %psum.7 = f32[256]{0:T(256)S(1)} all-reduce(f32[256]{0:T(256)S(1)} %get-tuple-element.66), channel_id=1, replica_groups=mesh['seq'=64,'tp'=8] {'tp'}, use_global_device_ids=true, to_apply=%region_11.12 | all-reduce | flops 256 | bytes 2048 | tf_op jit(solution)/shard_map/psum | solution.py:132
  (468 shorter events, 209.9 us)
Async XLA Ops:
  7.2 833.1 %all-gather.3.cloned.1.call-start = ((), (), s32[]{:S(2)}) async-start(), calls=%async_computation | async-start | bytes 14155776 | tf_op jit(solution)/shard_map/all_gather | solution.py:124
  45.1 10.0 %collective-permute-start = (bf16[2,256,384]{1,2,0:T(8,128)(2,1)}, bf16[2,256,384]{1,2,0:T(8,128)(2,1)S(1)}, u32[]{:S(2)}, u32[]{:S(2)}) collective-permute-start(bf16[2,256,384]{1,2,0:T(8,128)(2,1)} %get-tuple-element.159), channel_id=1, source_target_pairs={{0,8},{8,16},{16,24},{24,32},{32,40},{40,48},{48,56},{56,64},{64,7... | collective-permute-start | bytes 1179656 | tf_op jit(solution)/shard_map/while/body/eval_jaxpr/ppermute | solution.py:18
  56.9 10.0 %collective-permute-start = (bf16[2,256,384]{1,2,0:T(8,128)(2,1)}, bf16[2,256,384]{1,2,0:T(8,128)(2,1)S(1)}, u32[]{:S(2)}, u32[]{:S(2)}) collective-permute-start(bf16[2,256,384]{1,2,0:T(8,128)(2,1)} %get-tuple-element.159), channel_id=1, source_target_pairs={{0,8},{8,16},{16,24},{24,32},{32,40},{40,48},{48,56},{56,64},{64,7... | collective-permute-start | bytes 1179656 | tf_op jit(solution)/shard_map/while/body/eval_jaxpr/ppermute | solution.py:18
  68.7 10.0 %collective-permute-start = (bf16[2,256,384]{1,2,0:T(8,128)(2,1)}, bf16[2,256,384]{1,2,0:T(8,128)(2,1)S(1)}, u32[]{:S(2)}, u32[]{:S(2)}) collective-permute-start(bf16[2,256,384]{1,2,0:T(8,128)(2,1)} %get-tuple-element.159), channel_id=1, source_target_pairs={{0,8},{8,16},{16,24},{24,32},{32,40},{40,48},{48,56},{56,64},{64,7... | collective-permute-start | bytes 1179656 | tf_op jit(solution)/shard_map/while/body/eval_jaxpr/ppermute | solution.py:18
  80.5 10.0 %collective-permute-start = (bf16[2,256,384]{1,2,0:T(8,128)(2,1)}, bf16[2,256,384]{1,2,0:T(8,128)(2,1)S(1)}, u32[]{:S(2)}, u32[]{:S(2)}) collective-permute-start(bf16[2,256,384]{1,2,0:T(8,128)(2,1)} %get-tuple-element.159), channel_id=1, source_target_pairs={{0,8},{8,16},{16,24},{24,32},{32,40},{40,48},{48,56},{56,64},{64,7... | collective-permute-start | bytes 1179656 | tf_op jit(solution)/shard_map/while/body/eval_jaxpr/ppermute | solution.py:18
  92.4 10.0 %collective-permute-start = (bf16[2,256,384]{1,2,0:T(8,128)(2,1)}, bf16[2,256,384]{1,2,0:T(8,128)(2,1)S(1)}, u32[]{:S(2)}, u32[]{:S(2)}) collective-permute-start(bf16[2,256,384]{1,2,0:T(8,128)(2,1)} %get-tuple-element.159), channel_id=1, source_target_pairs={{0,8},{8,16},{16,24},{24,32},{32,40},{40,48},{48,56},{56,64},{64,7... | collective-permute-start | bytes 1179656 | tf_op jit(solution)/shard_map/while/body/eval_jaxpr/ppermute | solution.py:18
  104.2 10.0 %collective-permute-start = (bf16[2,256,384]{1,2,0:T(8,128)(2,1)}, bf16[2,256,384]{1,2,0:T(8,128)(2,1)S(1)}, u32[]{:S(2)}, u32[]{:S(2)}) collective-permute-start(bf16[2,256,384]{1,2,0:T(8,128)(2,1)} %get-tuple-element.159), channel_id=1, source_target_pairs={{0,8},{8,16},{16,24},{24,32},{32,40},{40,48},{48,56},{56,64},{64,7... | collective-permute-start | bytes 1179656 | tf_op jit(solution)/shard_map/while/body/eval_jaxpr/ppermute | solution.py:18
  116.0 10.0 %collective-permute-start = (bf16[2,256,384]{1,2,0:T(8,128)(2,1)}, bf16[2,256,384]{1,2,0:T(8,128)(2,1)S(1)}, u32[]{:S(2)}, u32[]{:S(2)}) collective-permute-start(bf16[2,256,384]{1,2,0:T(8,128)(2,1)} %get-tuple-element.159), channel_id=1, source_target_pairs={{0,8},{8,16},{16,24},{24,32},{32,40},{40,48},{48,56},{56,64},{64,7... | collective-permute-start | bytes 1179656 | tf_op jit(solution)/shard_map/while/body/eval_jaxpr/ppermute | solution.py:18
  127.8 10.0 %collective-permute-start = (bf16[2,256,384]{1,2,0:T(8,128)(2,1)}, bf16[2,256,384]{1,2,0:T(8,128)(2,1)S(1)}, u32[]{:S(2)}, u32[]{:S(2)}) collective-permute-start(bf16[2,256,384]{1,2,0:T(8,128)(2,1)} %get-tuple-element.159), channel_id=1, source_target_pairs={{0,8},{8,16},{16,24},{24,32},{32,40},{40,48},{48,56},{56,64},{64,7... | collective-permute-start | bytes 1179656 | tf_op jit(solution)/shard_map/while/body/eval_jaxpr/ppermute | solution.py:18
  139.6 10.0 %collective-permute-start = (bf16[2,256,384]{1,2,0:T(8,128)(2,1)}, bf16[2,256,384]{1,2,0:T(8,128)(2,1)S(1)}, u32[]{:S(2)}, u32[]{:S(2)}) collective-permute-start(bf16[2,256,384]{1,2,0:T(8,128)(2,1)} %get-tuple-element.159), channel_id=1, source_target_pairs={{0,8},{8,16},{16,24},{24,32},{32,40},{40,48},{48,56},{56,64},{64,7... | collective-permute-start | bytes 1179656 | tf_op jit(solution)/shard_map/while/body/eval_jaxpr/ppermute | solution.py:18
  151.5 10.0 %collective-permute-start = (bf16[2,256,384]{1,2,0:T(8,128)(2,1)}, bf16[2,256,384]{1,2,0:T(8,128)(2,1)S(1)}, u32[]{:S(2)}, u32[]{:S(2)}) collective-permute-start(bf16[2,256,384]{1,2,0:T(8,128)(2,1)} %get-tuple-element.159), channel_id=1, source_target_pairs={{0,8},{8,16},{16,24},{24,32},{32,40},{40,48},{48,56},{56,64},{64,7... | collective-permute-start | bytes 1179656 | tf_op jit(solution)/shard_map/while/body/eval_jaxpr/ppermute | solution.py:18
  163.3 15.6 %collective-permute-start = (bf16[2,256,384]{1,2,0:T(8,128)(2,1)}, bf16[2,256,384]{1,2,0:T(8,128)(2,1)S(1)}, u32[]{:S(2)}, u32[]{:S(2)}) collective-permute-start(bf16[2,256,384]{1,2,0:T(8,128)(2,1)} %get-tuple-element.159), channel_id=1, source_target_pairs={{0,8},{8,16},{16,24},{24,32},{32,40},{40,48},{48,56},{56,64},{64,7... | collective-permute-start | bytes 1179656 | tf_op jit(solution)/shard_map/while/body/eval_jaxpr/ppermute | solution.py:18
  166.1 12.1 %collective-permute-start.1 = (s32[256]{0:T(256)}, s32[256]{0:T(256)S(1)}, u32[]{:S(2)}, u32[]{:S(2)}) collective-permute-start(s32[256]{0:T(256)} %get-tuple-element.160), channel_id=1, source_target_pairs={{0,8},{8,16},{16,24},{24,32},{32,40},{40,48},{48,56},{56,64},{64,7... | collective-permute-start | bytes 3080 | tf_op jit(solution)/shard_map/while/body/eval_jaxpr/ppermute | solution.py:18
  180.7 17.1 %collective-permute-start = (bf16[2,256,384]{1,2,0:T(8,128)(2,1)}, bf16[2,256,384]{1,2,0:T(8,128)(2,1)S(1)}, u32[]{:S(2)}, u32[]{:S(2)}) collective-permute-start(bf16[2,256,384]{1,2,0:T(8,128)(2,1)} %get-tuple-element.159), channel_id=1, source_target_pairs={{0,8},{8,16},{16,24},{24,32},{32,40},{40,48},{48,56},{56,64},{64,7... | collective-permute-start | bytes 1179656 | tf_op jit(solution)/shard_map/while/body/eval_jaxpr/ppermute | solution.py:18
  184.7 12.4 %collective-permute-start.1 = (s32[256]{0:T(256)}, s32[256]{0:T(256)S(1)}, u32[]{:S(2)}, u32[]{:S(2)}) collective-permute-start(s32[256]{0:T(256)} %get-tuple-element.160), channel_id=1, source_target_pairs={{0,8},{8,16},{16,24},{24,32},{32,40},{40,48},{48,56},{56,64},{64,7... | collective-permute-start | bytes 3080 | tf_op jit(solution)/shard_map/while/body/eval_jaxpr/ppermute | solution.py:18
  199.6 16.3 %collective-permute-start = (bf16[2,256,384]{1,2,0:T(8,128)(2,1)}, bf16[2,256,384]{1,2,0:T(8,128)(2,1)S(1)}, u32[]{:S(2)}, u32[]{:S(2)}) collective-permute-start(bf16[2,256,384]{1,2,0:T(8,128)(2,1)} %get-tuple-element.159), channel_id=1, source_target_pairs={{0,8},{8,16},{16,24},{24,32},{32,40},{40,48},{48,56},{56,64},{64,7... | collective-permute-start | bytes 1179656 | tf_op jit(solution)/shard_map/while/body/eval_jaxpr/ppermute | solution.py:18
  203.6 11.6 %collective-permute-start.1 = (s32[256]{0:T(256)}, s32[256]{0:T(256)S(1)}, u32[]{:S(2)}, u32[]{:S(2)}) collective-permute-start(s32[256]{0:T(256)} %get-tuple-element.160), channel_id=1, source_target_pairs={{0,8},{8,16},{16,24},{24,32},{32,40},{40,48},{48,56},{56,64},{64,7... | collective-permute-start | bytes 3080 | tf_op jit(solution)/shard_map/while/body/eval_jaxpr/ppermute | solution.py:18
  217.7 14.9 %collective-permute-start = (bf16[2,256,384]{1,2,0:T(8,128)(2,1)}, bf16[2,256,384]{1,2,0:T(8,128)(2,1)S(1)}, u32[]{:S(2)}, u32[]{:S(2)}) collective-permute-start(bf16[2,256,384]{1,2,0:T(8,128)(2,1)} %get-tuple-element.159), channel_id=1, source_target_pairs={{0,8},{8,16},{16,24},{24,32},{32,40},{40,48},{48,56},{56,64},{64,7... | collective-permute-start | bytes 1179656 | tf_op jit(solution)/shard_map/while/body/eval_jaxpr/ppermute | solution.py:18
  221.7 10.3 %collective-permute-start.1 = (s32[256]{0:T(256)}, s32[256]{0:T(256)S(1)}, u32[]{:S(2)}, u32[]{:S(2)}) collective-permute-start(s32[256]{0:T(256)} %get-tuple-element.160), channel_id=1, source_target_pairs={{0,8},{8,16},{16,24},{24,32},{32,40},{40,48},{48,56},{56,64},{64,7... | collective-permute-start | bytes 3080 | tf_op jit(solution)/shard_map/while/body/eval_jaxpr/ppermute | solution.py:18
  234.4 13.0 %collective-permute-start = (bf16[2,256,384]{1,2,0:T(8,128)(2,1)}, bf16[2,256,384]{1,2,0:T(8,128)(2,1)S(1)}, u32[]{:S(2)}, u32[]{:S(2)}) collective-permute-start(bf16[2,256,384]{1,2,0:T(8,128)(2,1)} %get-tuple-element.159), channel_id=1, source_target_pairs={{0,8},{8,16},{16,24},{24,32},{32,40},{40,48},{48,56},{56,64},{64,7... | collective-permute-start | bytes 1179656 | tf_op jit(solution)/shard_map/while/body/eval_jaxpr/ppermute | solution.py:18
  249.3 13.0 %collective-permute-start = (bf16[2,256,384]{1,2,0:T(8,128)(2,1)}, bf16[2,256,384]{1,2,0:T(8,128)(2,1)S(1)}, u32[]{:S(2)}, u32[]{:S(2)}) collective-permute-start(bf16[2,256,384]{1,2,0:T(8,128)(2,1)} %get-tuple-element.159), channel_id=1, source_target_pairs={{0,8},{8,16},{16,24},{24,32},{32,40},{40,48},{48,56},{56,64},{64,7... | collective-permute-start | bytes 1179656 | tf_op jit(solution)/shard_map/while/body/eval_jaxpr/ppermute | solution.py:18
  264.1 13.0 %collective-permute-start = (bf16[2,256,384]{1,2,0:T(8,128)(2,1)}, bf16[2,256,384]{1,2,0:T(8,128)(2,1)S(1)}, u32[]{:S(2)}, u32[]{:S(2)}) collective-permute-start(bf16[2,256,384]{1,2,0:T(8,128)(2,1)} %get-tuple-element.159), channel_id=1, source_target_pairs={{0,8},{8,16},{16,24},{24,32},{32,40},{40,48},{48,56},{56,64},{64,7... | collective-permute-start | bytes 1179656 | tf_op jit(solution)/shard_map/while/body/eval_jaxpr/ppermute | solution.py:18
  278.9 13.0 %collective-permute-start = (bf16[2,256,384]{1,2,0:T(8,128)(2,1)}, bf16[2,256,384]{1,2,0:T(8,128)(2,1)S(1)}, u32[]{:S(2)}, u32[]{:S(2)}) collective-permute-start(bf16[2,256,384]{1,2,0:T(8,128)(2,1)} %get-tuple-element.159), channel_id=1, source_target_pairs={{0,8},{8,16},{16,24},{24,32},{32,40},{40,48},{48,56},{56,64},{64,7... | collective-permute-start | bytes 1179656 | tf_op jit(solution)/shard_map/while/body/eval_jaxpr/ppermute | solution.py:18
  293.8 13.7 %collective-permute-start = (bf16[2,256,384]{1,2,0:T(8,128)(2,1)}, bf16[2,256,384]{1,2,0:T(8,128)(2,1)S(1)}, u32[]{:S(2)}, u32[]{:S(2)}) collective-permute-start(bf16[2,256,384]{1,2,0:T(8,128)(2,1)} %get-tuple-element.159), channel_id=1, source_target_pairs={{0,8},{8,16},{16,24},{24,32},{32,40},{40,48},{48,56},{56,64},{64,7... | collective-permute-start | bytes 1179656 | tf_op jit(solution)/shard_map/while/body/eval_jaxpr/ppermute | solution.py:18
  297.8 9.1 %collective-permute-start.1 = (s32[256]{0:T(256)}, s32[256]{0:T(256)S(1)}, u32[]{:S(2)}, u32[]{:S(2)}) collective-permute-start(s32[256]{0:T(256)} %get-tuple-element.160), channel_id=1, source_target_pairs={{0,8},{8,16},{16,24},{24,32},{32,40},{40,48},{48,56},{56,64},{64,7... | collective-permute-start | bytes 3080 | tf_op jit(solution)/shard_map/while/body/eval_jaxpr/ppermute | solution.py:18
  309.3 13.7 %collective-permute-start = (bf16[2,256,384]{1,2,0:T(8,128)(2,1)}, bf16[2,256,384]{1,2,0:T(8,128)(2,1)S(1)}, u32[]{:S(2)}, u32[]{:S(2)}) collective-permute-start(bf16[2,256,384]{1,2,0:T(8,128)(2,1)} %get-tuple-element.159), channel_id=1, source_target_pairs={{0,8},{8,16},{16,24},{24,32},{32,40},{40,48},{48,56},{56,64},{64,7... | collective-permute-start | bytes 1179656 | tf_op jit(solution)/shard_map/while/body/eval_jaxpr/ppermute | solution.py:18
  313.3 9.0 %collective-permute-start.1 = (s32[256]{0:T(256)}, s32[256]{0:T(256)S(1)}, u32[]{:S(2)}, u32[]{:S(2)}) collective-permute-start(s32[256]{0:T(256)} %get-tuple-element.160), channel_id=1, source_target_pairs={{0,8},{8,16},{16,24},{24,32},{32,40},{40,48},{48,56},{56,64},{64,7... | collective-permute-start | bytes 3080 | tf_op jit(solution)/shard_map/while/body/eval_jaxpr/ppermute | solution.py:18
  324.9 13.7 %collective-permute-start = (bf16[2,256,384]{1,2,0:T(8,128)(2,1)}, bf16[2,256,384]{1,2,0:T(8,128)(2,1)S(1)}, u32[]{:S(2)}, u32[]{:S(2)}) collective-permute-start(bf16[2,256,384]{1,2,0:T(8,128)(2,1)} %get-tuple-element.159), channel_id=1, source_target_pairs={{0,8},{8,16},{16,24},{24,32},{32,40},{40,48},{48,56},{56,64},{64,7... | collective-permute-start | bytes 1179656 | tf_op jit(solution)/shard_map/while/body/eval_jaxpr/ppermute | solution.py:18
  328.9 9.0 %collective-permute-start.1 = (s32[256]{0:T(256)}, s32[256]{0:T(256)S(1)}, u32[]{:S(2)}, u32[]{:S(2)}) collective-permute-start(s32[256]{0:T(256)} %get-tuple-element.160), channel_id=1, source_target_pairs={{0,8},{8,16},{16,24},{24,32},{32,40},{40,48},{48,56},{56,64},{64,7... | collective-permute-start | bytes 3080 | tf_op jit(solution)/shard_map/while/body/eval_jaxpr/ppermute | solution.py:18
  340.4 13.7 %collective-permute-start = (bf16[2,256,384]{1,2,0:T(8,128)(2,1)}, bf16[2,256,384]{1,2,0:T(8,128)(2,1)S(1)}, u32[]{:S(2)}, u32[]{:S(2)}) collective-permute-start(bf16[2,256,384]{1,2,0:T(8,128)(2,1)} %get-tuple-element.159), channel_id=1, source_target_pairs={{0,8},{8,16},{16,24},{24,32},{32,40},{40,48},{48,56},{56,64},{64,7... | collective-permute-start | bytes 1179656 | tf_op jit(solution)/shard_map/while/body/eval_jaxpr/ppermute | solution.py:18
  344.4 9.0 %collective-permute-start.1 = (s32[256]{0:T(256)}, s32[256]{0:T(256)S(1)}, u32[]{:S(2)}, u32[]{:S(2)}) collective-permute-start(s32[256]{0:T(256)} %get-tuple-element.160), channel_id=1, source_target_pairs={{0,8},{8,16},{16,24},{24,32},{32,40},{40,48},{48,56},{56,64},{64,7... | collective-permute-start | bytes 3080 | tf_op jit(solution)/shard_map/while/body/eval_jaxpr/ppermute | solution.py:18
  355.9 13.7 %collective-permute-start = (bf16[2,256,384]{1,2,0:T(8,128)(2,1)}, bf16[2,256,384]{1,2,0:T(8,128)(2,1)S(1)}, u32[]{:S(2)}, u32[]{:S(2)}) collective-permute-start(bf16[2,256,384]{1,2,0:T(8,128)(2,1)} %get-tuple-element.159), channel_id=1, source_target_pairs={{0,8},{8,16},{16,24},{24,32},{32,40},{40,48},{48,56},{56,64},{64,7... | collective-permute-start | bytes 1179656 | tf_op jit(solution)/shard_map/while/body/eval_jaxpr/ppermute | solution.py:18
  359.9 9.0 %collective-permute-start.1 = (s32[256]{0:T(256)}, s32[256]{0:T(256)S(1)}, u32[]{:S(2)}, u32[]{:S(2)}) collective-permute-start(s32[256]{0:T(256)} %get-tuple-element.160), channel_id=1, source_target_pairs={{0,8},{8,16},{16,24},{24,32},{32,40},{40,48},{48,56},{56,64},{64,7... | collective-permute-start | bytes 3080 | tf_op jit(solution)/shard_map/while/body/eval_jaxpr/ppermute | solution.py:18
  371.4 13.7 %collective-permute-start = (bf16[2,256,384]{1,2,0:T(8,128)(2,1)}, bf16[2,256,384]{1,2,0:T(8,128)(2,1)S(1)}, u32[]{:S(2)}, u32[]{:S(2)}) collective-permute-start(bf16[2,256,384]{1,2,0:T(8,128)(2,1)} %get-tuple-element.159), channel_id=1, source_target_pairs={{0,8},{8,16},{16,24},{24,32},{32,40},{40,48},{48,56},{56,64},{64,7... | collective-permute-start | bytes 1179656 | tf_op jit(solution)/shard_map/while/body/eval_jaxpr/ppermute | solution.py:18
  375.4 9.0 %collective-permute-start.1 = (s32[256]{0:T(256)}, s32[256]{0:T(256)S(1)}, u32[]{:S(2)}, u32[]{:S(2)}) collective-permute-start(s32[256]{0:T(256)} %get-tuple-element.160), channel_id=1, source_target_pairs={{0,8},{8,16},{16,24},{24,32},{32,40},{40,48},{48,56},{56,64},{64,7... | collective-permute-start | bytes 3080 | tf_op jit(solution)/shard_map/while/body/eval_jaxpr/ppermute | solution.py:18
  386.9 13.7 %collective-permute-start = (bf16[2,256,384]{1,2,0:T(8,128)(2,1)}, bf16[2,256,384]{1,2,0:T(8,128)(2,1)S(1)}, u32[]{:S(2)}, u32[]{:S(2)}) collective-permute-start(bf16[2,256,384]{1,2,0:T(8,128)(2,1)} %get-tuple-element.159), channel_id=1, source_target_pairs={{0,8},{8,16},{16,24},{24,32},{32,40},{40,48},{48,56},{56,64},{64,7... | collective-permute-start | bytes 1179656 | tf_op jit(solution)/shard_map/while/body/eval_jaxpr/ppermute | solution.py:18
  390.9 9.0 %collective-permute-start.1 = (s32[256]{0:T(256)}, s32[256]{0:T(256)S(1)}, u32[]{:S(2)}, u32[]{:S(2)}) collective-permute-start(s32[256]{0:T(256)} %get-tuple-element.160), channel_id=1, source_target_pairs={{0,8},{8,16},{16,24},{24,32},{32,40},{40,48},{48,56},{56,64},{64,7... | collective-permute-start | bytes 3080 | tf_op jit(solution)/shard_map/while/body/eval_jaxpr/ppermute | solution.py:18
  402.5 13.7 %collective-permute-start = (bf16[2,256,384]{1,2,0:T(8,128)(2,1)}, bf16[2,256,384]{1,2,0:T(8,128)(2,1)S(1)}, u32[]{:S(2)}, u32[]{:S(2)}) collective-permute-start(bf16[2,256,384]{1,2,0:T(8,128)(2,1)} %get-tuple-element.159), channel_id=1, source_target_pairs={{0,8},{8,16},{16,24},{24,32},{32,40},{40,48},{48,56},{56,64},{64,7... | collective-permute-start | bytes 1179656 | tf_op jit(solution)/shard_map/while/body/eval_jaxpr/ppermute | solution.py:18
  406.4 9.0 %collective-permute-start.1 = (s32[256]{0:T(256)}, s32[256]{0:T(256)S(1)}, u32[]{:S(2)}, u32[]{:S(2)}) collective-permute-start(s32[256]{0:T(256)} %get-tuple-element.160), channel_id=1, source_target_pairs={{0,8},{8,16},{16,24},{24,32},{32,40},{40,48},{48,56},{56,64},{64,7... | collective-permute-start | bytes 3080 | tf_op jit(solution)/shard_map/while/body/eval_jaxpr/ppermute | solution.py:18
  418.0 13.7 %collective-permute-start = (bf16[2,256,384]{1,2,0:T(8,128)(2,1)}, bf16[2,256,384]{1,2,0:T(8,128)(2,1)S(1)}, u32[]{:S(2)}, u32[]{:S(2)}) collective-permute-start(bf16[2,256,384]{1,2,0:T(8,128)(2,1)} %get-tuple-element.159), channel_id=1, source_target_pairs={{0,8},{8,16},{16,24},{24,32},{32,40},{40,48},{48,56},{56,64},{64,7... | collective-permute-start | bytes 1179656 | tf_op jit(solution)/shard_map/while/body/eval_jaxpr/ppermute | solution.py:18
  433.5 13.7 %collective-permute-start = (bf16[2,256,384]{1,2,0:T(8,128)(2,1)}, bf16[2,256,384]{1,2,0:T(8,128)(2,1)S(1)}, u32[]{:S(2)}, u32[]{:S(2)}) collective-permute-start(bf16[2,256,384]{1,2,0:T(8,128)(2,1)} %get-tuple-element.159), channel_id=1, source_target_pairs={{0,8},{8,16},{16,24},{24,32},{32,40},{40,48},{48,56},{56,64},{64,7... | collective-permute-start | bytes 1179656 | tf_op jit(solution)/shard_map/while/body/eval_jaxpr/ppermute | solution.py:18
  449.0 13.7 %collective-permute-start = (bf16[2,256,384]{1,2,0:T(8,128)(2,1)}, bf16[2,256,384]{1,2,0:T(8,128)(2,1)S(1)}, u32[]{:S(2)}, u32[]{:S(2)}) collective-permute-start(bf16[2,256,384]{1,2,0:T(8,128)(2,1)} %get-tuple-element.159), channel_id=1, source_target_pairs={{0,8},{8,16},{16,24},{24,32},{32,40},{40,48},{48,56},{56,64},{64,7... | collective-permute-start | bytes 1179656 | tf_op jit(solution)/shard_map/while/body/eval_jaxpr/ppermute | solution.py:18
  464.5 13.7 %collective-permute-start = (bf16[2,256,384]{1,2,0:T(8,128)(2,1)}, bf16[2,256,384]{1,2,0:T(8,128)(2,1)S(1)}, u32[]{:S(2)}, u32[]{:S(2)}) collective-permute-start(bf16[2,256,384]{1,2,0:T(8,128)(2,1)} %get-tuple-element.159), channel_id=1, source_target_pairs={{0,8},{8,16},{16,24},{24,32},{32,40},{40,48},{48,56},{56,64},{64,7... | collective-permute-start | bytes 1179656 | tf_op jit(solution)/shard_map/while/body/eval_jaxpr/ppermute | solution.py:18
  468.5 9.0 %collective-permute-start.1 = (s32[256]{0:T(256)}, s32[256]{0:T(256)S(1)}, u32[]{:S(2)}, u32[]{:S(2)}) collective-permute-start(s32[256]{0:T(256)} %get-tuple-element.160), channel_id=1, source_target_pairs={{0,8},{8,16},{16,24},{24,32},{32,40},{40,48},{48,56},{56,64},{64,7... | collective-permute-start | bytes 3080 | tf_op jit(solution)/shard_map/while/body/eval_jaxpr/ppermute | solution.py:18
  480.0 13.7 %collective-permute-start = (bf16[2,256,384]{1,2,0:T(8,128)(2,1)}, bf16[2,256,384]{1,2,0:T(8,128)(2,1)S(1)}, u32[]{:S(2)}, u32[]{:S(2)}) collective-permute-start(bf16[2,256,384]{1,2,0:T(8,128)(2,1)} %get-tuple-element.159), channel_id=1, source_target_pairs={{0,8},{8,16},{16,24},{24,32},{32,40},{40,48},{48,56},{56,64},{64,7... | collective-permute-start | bytes 1179656 | tf_op jit(solution)/shard_map/while/body/eval_jaxpr/ppermute | solution.py:18
  484.0 9.0 %collective-permute-start.1 = (s32[256]{0:T(256)}, s32[256]{0:T(256)S(1)}, u32[]{:S(2)}, u32[]{:S(2)}) collective-permute-start(s32[256]{0:T(256)} %get-tuple-element.160), channel_id=1, source_target_pairs={{0,8},{8,16},{16,24},{24,32},{32,40},{40,48},{48,56},{56,64},{64,7... | collective-permute-start | bytes 3080 | tf_op jit(solution)/shard_map/while/body/eval_jaxpr/ppermute | solution.py:18
  495.5 13.7 %collective-permute-start = (bf16[2,256,384]{1,2,0:T(8,128)(2,1)}, bf16[2,256,384]{1,2,0:T(8,128)(2,1)S(1)}, u32[]{:S(2)}, u32[]{:S(2)}) collective-permute-start(bf16[2,256,384]{1,2,0:T(8,128)(2,1)} %get-tuple-element.159), channel_id=1, source_target_pairs={{0,8},{8,16},{16,24},{24,32},{32,40},{40,48},{48,56},{56,64},{64,7... | collective-permute-start | bytes 1179656 | tf_op jit(solution)/shard_map/while/body/eval_jaxpr/ppermute | solution.py:18
  499.5 9.0 %collective-permute-start.1 = (s32[256]{0:T(256)}, s32[256]{0:T(256)S(1)}, u32[]{:S(2)}, u32[]{:S(2)}) collective-permute-start(s32[256]{0:T(256)} %get-tuple-element.160), channel_id=1, source_target_pairs={{0,8},{8,16},{16,24},{24,32},{32,40},{40,48},{48,56},{56,64},{64,7... | collective-permute-start | bytes 3080 | tf_op jit(solution)/shard_map/while/body/eval_jaxpr/ppermute | solution.py:18
  (30 other events, 1078.9 us)
Sparse Core Ops, SparseCore 0:
  513.4 326.8 all-gather.2
